TPU v7x, 256 devices: a whole 4x4x8 slice. The times are simulated.
256 devices in a mesh: tm: 32 (over y, x, core), tensor: 8 (over z).
Axes of the slice: x: 4, y: 4, z: 8, core: 2. Of those that a mesh axis runs over, the one named last changes fastest.
Arguments:
- features: bfloat16 [32768, 1536], P(('tm', 'tensor')), may hold values from -4 to 4
- frame_mask: int32 [32768], P('tm'), may hold values 0 or 1
- total_length: int32 [1], replicated, may hold values from 24576 to 32768
- norm_gain: float32 [1536], replicated, may hold values from 0.1 to 1.9
- value_weight: bfloat16 [1536, 1536], P(None, 'tensor'), may hold values from -0.15625 to 0.15625
- gate_weight: bfloat16 [1536, 1536], P(None, 'tensor'), may hold values from -0.15625 to 0.15625
- depth_kernel: float32 [31, 1536], P(None, 'tensor'), may hold values from -1 to 1
- batch_gain: float32 [1536], P('tensor'), may hold values from 0.1 to 1.9
- batch_bias: float32 [1536], P('tensor'), may hold values from -2 to 2
- out_weight: bfloat16 [1536, 1536], P('tensor'), may hold values from -0.15625 to 0.15625
- feed_gain: float32 [1536], replicated, may hold values from 0.1 to 1.9
- up_weight: bfloat16 [1536, 6144], P('tm', 'tensor'), may hold values from -0.15625 to 0.15625
- down_weight: bfloat16 [6144, 1536], P('tensor', 'tm'), may hold values from -0.078125 to 0.078125
Outputs:
- encoded: bfloat16 [32768, 1536], P(('tm', 'tensor'))
All inputs are finite; a program needn't handle non-finite values. No bound on the sum of `frame_mask` on one device may be relied on, other than what follows from the above.
Results may differ from a plain program's by a relative error of at most 0.0074.
Values may be sent and summed in bfloat16 or wider, within the bound.
No kernel may reach another device: no remote copies, remote signals or barrier semaphores. Data moves between devices by JAX's collectives and lax.ppermute only.
A program may use at most 64 MiB of HBM per device.

v0:
```python
import jax
import jax.numpy as jnp
from jax import lax
from jax.sharding import PartitionSpec as P

KERNEL = 31


def extended(array, sides, width):
    for axis, dim in sides:
        devices, length = (lax.axis_size(axis), array.shape[dim])
        up = [(i, (i + 1) % devices) for i in range(devices - 1)]
        down = [(j, i) for i, j in up]
        last = lax.slice_in_dim(array, length - width, length, axis=dim)
        initial = lax.slice_in_dim(array, 0, width, axis=dim)
        before = lax.ppermute(last, axis, up)
        after = lax.ppermute(initial, axis, down)
        array = jnp.concatenate([before, array, after], axis=dim)
    return array


def layer_norm(rows, gain):
    values = rows.astype(jnp.float32)
    centre = jnp.mean(values, axis=-1, keepdims=True)
    spread = jnp.mean(jnp.square(values - centre), axis=-1, keepdims=True)
    return (values - centre) * lax.rsqrt(spread + 1e-05) * gain


def shards(
    features,
    frame_mask,
    total_length,
    norm_gain,
    value_weight,
    gate_weight,
    depth_kernel,
    batch_gain,
    batch_bias,
    out_weight,
    feed_gain,
    up_weight,
    down_weight,
):
    own_rows = features.shape[0]
    block = own_rows * lax.axis_size("tensor")
    positions = lax.axis_index("tm") * block + jnp.arange(block, dtype=jnp.int32)
    valid = ((frame_mask > 0) & (positions < total_length[0])).astype(jnp.float32)
    normed = layer_norm(features, norm_gain).astype(jnp.bfloat16)
    piece = lax.all_gather(normed, "tensor", axis=0, tiled=True)
    value = jnp.dot(piece, value_weight, preferred_element_type=jnp.float32)
    gate = jnp.dot(piece, gate_weight, preferred_element_type=jnp.float32)
    glu = (value * jax.nn.sigmoid(gate) * valid[:, None]).astype(jnp.bfloat16)
    padded = extended(glu, (("tm", 0),), KERNEL // 2)
    conv = jnp.zeros(glu.shape, jnp.float32)
    for tap in range(KERNEL):
        conv = conv + padded[tap : tap + block].astype(jnp.float32) * depth_kernel[tap]
    count_local = jnp.sum(valid)
    first_sum = jnp.sum(conv * valid[:, None], axis=0)
    total, count = lax.psum((first_sum, count_local), "tm")
    mean = total / count
    centred = conv - mean
    spread = lax.psum(jnp.sum(jnp.square(centred) * valid[:, None], axis=0), "tm")
    var = spread / count
    scaled = centred * lax.rsqrt(var + 1e-05) * batch_gain + batch_bias
    swished = (scaled * jax.nn.sigmoid(scaled)).astype(jnp.bfloat16)
    conv_out = lax.psum_scatter(
        jnp.dot(swished, out_weight, preferred_element_type=jnp.float32),
        "tensor",
        scatter_dimension=0,
        tiled=True,
    )
    mid = (features.astype(jnp.float32) + conv_out).astype(jnp.bfloat16)
    feed_normed = layer_norm(mid, feed_gain).astype(jnp.bfloat16)
    feed_block = lax.all_gather(feed_normed, "tensor", axis=0, tiled=True)
    up_whole = lax.all_gather(up_weight, "tm", axis=0, tiled=True)
    pre = jnp.dot(feed_block, up_whole, preferred_element_type=jnp.float32)
    hidden = (pre * jax.nn.sigmoid(pre)).astype(jnp.bfloat16)
    down_whole = lax.all_gather(down_weight, "tm", axis=1, tiled=True)
    partial_out = jnp.dot(hidden, down_whole, preferred_element_type=jnp.float32)
    feed_out = lax.psum_scatter(partial_out, "tensor", scatter_dimension=0, tiled=True)
    return (mid.astype(jnp.float32) + 0.5 * feed_out).astype(jnp.bfloat16)


def solution(mesh):
    placed = (
        P(("tm", "tensor"), None),
        P("tm"),
        P(),
        P(),
        P(None, "tensor"),
        P(None, "tensor"),
        P(None, "tensor"),
        P("tensor"),
        P("tensor"),
        P("tensor", None),
        P(),
        P("tm", "tensor"),
        P("tensor", "tm"),
    )
    return jax.shard_map(
        shards, mesh=mesh, in_specs=placed, out_specs=P(("tm", "tensor"), None), check_vma=False
    )
```

profile of v0, /device:TPU:1, one launch (start us, length us, event | category | flops | bytes accessed | tf_op | source)
XLA Modules:
  0.0 450.7 jit_solution(13662535378616291768)
XLA Ops:
  7.4 1.2 convert_reduce_fusion.1
  8.6 1.2 fusion.14
  9.8 2.0 fusion.16
  12.6 1.4 fusion.58
  14.0 1.0 fusion.61
  15.0 45.6 %all-gather.5.cloned.1.call-done = bf16[1024,1536]{1,0:T(8,128)(2,1)} async-done(((bf16[128,1536]{1,0:T(8,128)(2,1)}), bf16[1024,1536]{1,0:T(8,128)(2,1)}) %all-gather.5.cloned.1.call-update) | async-done | bytes 3145744 | tf_op jit(solution)/shard_map/all_gather | solution.py:49
  60.6 3.4 fusion.5
  64.0 1.2 fusion.6
  65.3 3.9 collective-permute-start
  69.2 1.9 collective-permute-start.1
  71.1 1.0 fusion.62
  72.1 2.5 collective-permute-done.1
  74.6 5.6 %multiply_reduce_fusion.1 = (f32[192]{0:T(256)S(1)}, f32[1024,192]{0,1:T(8,128)S(1)}) fusion(f32[1024]{0:T(1024)S(1)} %get-tuple-element.10, f32[192]{0:T(256)S(1)} %bitcast.70, bf16[15,192]{0,1:T(8,128)(2,1)S(1)} %collective-permute-done.1, bf16[1024,192]{0,1:T(8,128)(2,1)S(1)} %fusion.6, f32[192]{0:T(256)S(1)} %bitcast.71, f32[192]{0:T(256)S(1)} %bitcast.42, ...), kind=kLoop, calls=%fused_computation.58 | loop fusion | flops 36175680 | bytes 1219840 | tf_op jit(solution)/shard_map/reduce_sum | solution.py:58
  80.2 61.4 %all-reduce = (f32[192]{0:T(256)S(1)}, f32[]{:T(128)}) all-reduce(f32[192]{0:T(256)S(1)} %get-tuple-element.11, f32[]{:T(128)} %get-tuple-element.9), channel_id=1, replica_groups=mesh['tm'=32,'tensor'=8] {'tm'}, use_global_device_ids=true, to_apply=%region_3.0 | all-reduce | flops 193 | bytes 1544 | tf_op jit(solution)/shard_map/psum | solution.py:59
  142.5 65.3 %psum.23 = f32[192]{0:T(256)S(1)} all-reduce(f32[192]{0:T(256)S(1)} %multiply_reduce_fusion), channel_id=1, replica_groups=mesh['tm'=32,'tensor'=8] {'tm'}, use_global_device_ids=true, to_apply=%region_7.0 | all-reduce | flops 192 | bytes 1536 | tf_op jit(solution)/shard_map/psum | solution.py:62
  208.4 3.9 fusion.19
  213.6 67.8 %reduce-scatter.3.cloned.1.call-done = f32[128,1536]{1,0:T(8,128)} async-done(((f32[1024,1536]{1,0:T(8,128)}), f32[128,1536]{1,0:T(8,128)}) %reduce-scatter.3.cloned.1.call-update) | async-done | bytes 786448 | tf_op jit(solution)/shard_map/reduce_scatter | solution.py:66
  281.4 1.3 convert_reduce_fusion
  283.0 1.0 fusion.13
  284.3 25.3 %all-gather.11.cloned.1.call-done = bf16[768,1536]{0,1:T(8,128)(2,1)} async-done(((bf16[768,48]{0,1:T(8,128)(2,1)}), bf16[768,1536]{0,1:T(8,128)(2,1)}) %all-gather.11.cloned.1.call-update) | async-done | bytes 2359312 | tf_op jit(solution)/shard_map/all_gather | solution.py:78
  309.6 45.3 %all-gather.7.cloned.1.call-done = bf16[1024,1536]{1,0:T(8,128)(2,1)} async-done(((bf16[128,1536]{1,0:T(8,128)(2,1)}), bf16[1024,1536]{1,0:T(8,128)(2,1)}) %all-gather.7.cloned.1.call-update) | async-done | bytes 3145744 | tf_op jit(solution)/shard_map/all_gather | solution.py:74
  354.9 12.1 %fusion = f32[1024,1536]{1,0:T(8,128)} fusion(bf16[768,1536]{0,1:T(8,128)(2,1)} %all-gather.11.cloned.1.call-done, bf16[1024,1536]{1,0:T(8,128)(2,1)} %all-gather.7.cloned.1.call-done, bf16[1536,768]{1,0:T(8,128)(2,1)} %all-gather.9.cloned.1.call-done), kind=kOutput, calls=%fused_computation.29 | convolution fusion | flops 4835770368 | bytes 14155776 | tf_op jit(solution)/shard_map/dot_general | solution.py:79
  367.0 74.2 %reduce-scatter.5.cloned.1.call-done = f32[128,1536]{1,0:T(8,128)} async-done(((f32[1024,1536]{1,0:T(8,128)}), f32[128,1536]{1,0:T(8,128)}) %reduce-scatter.5.cloned.1.call-update) | async-done | bytes 786448 | tf_op jit(solution)/shard_map/reduce_scatter | solution.py:80
  441.2 2.0 fusion.18
  (37 shorter events, 3.5 us)
Async XLA Ops:
  7.4 201.1 %copy-start = (bf16[192,1536]{1,0:T(8,128)(2,1)S(1)}, bf16[192,1536]{1,0:T(8,128)(2,1)}, u32[]{:S(2)}) copy-start(bf16[192,1536]{1,0:T(8,128)(2,1)} %param.22) | copy-start | bytes 1769476
  7.4 53.2 %all-gather.5.cloned.1.call-start = ((), (), s32[]{:S(2)}) async-start(), calls=%async_computation.2 | async-start | bytes 3538944 | tf_op jit(solution)/shard_map/all_gather | solution.py:49
  11.9 269.5 %reduce-scatter.3.cloned.1.call-start = ((), (), s32[]{:S(2)}) async-start(), calls=%async_computation.3 | async-start | bytes 7077888 | tf_op jit(solution)/shard_map/reduce_scatter | solution.py:66
  15.0 49.0 %copy-start.6 = (bf16[1536,192]{0,1:T(8,128)(2,1)S(1)}, bf16[1536,192]{0,1:T(8,128)(2,1)}, u32[]{:S(2)}) copy-start(bf16[1536,192]{0,1:T(8,128)(2,1)} %param.17) | copy-start | bytes 1769476
  60.6 3.4 copy-start.5
  64.0 144.4 %copy-start.3 = (f32[192]{0:T(256)S(1)}, f32[192]{0:T(256)}, u32[]{:S(2)}) copy-start(f32[192]{0:T(256)} %param.21) | copy-start | bytes 2308
  64.0 144.4 %copy-start.4 = (f32[192]{0:T(256)S(1)}, f32[192]{0:T(256)}, u32[]{:S(2)}) copy-start(f32[192]{0:T(256)} %param.20) | copy-start | bytes 2308
  65.3 6.8 %collective-permute-start = (bf16[15,192]{0,1:T(8,128)(2,1)S(1)}, bf16[15,192]{0,1:T(8,128)(2,1)S(1)}, u32[]{:S(2)}, u32[]{:S(2)}) collective-permute-start(bf16[15,192]{0,1:T(8,128)(2,1)S(1)} %get-tuple-element.13), channel_id=1, source_target_pairs={{0,8},{8,16},{16,24},{24,32},{32,40},{40,48},{48,56},{56,64},{64,7... | collective-permute-start | bytes 17288 | tf_op jit(solution)/shard_map/ppermute | solution.py:16
  69.2 5.4 %collective-permute-start.1 = (bf16[15,192]{0,1:T(8,128)(2,1)S(1)}, bf16[15,192]{0,1:T(8,128)(2,1)S(1)}, u32[]{:S(2)}, u32[]{:S(2)}) collective-permute-start(bf16[15,192]{0,1:T(8,128)(2,1)S(1)} %get-tuple-element.14), channel_id=1, source_target_pairs={{8,0},{16,8},{24,16},{32,24},{40,32},{48,40},{56,48},{64,56},{72,6... | collective-permute-start | bytes 17288 | tf_op jit(solution)/shard_map/ppermute | solution.py:17
  212.3 69.1 %copy-start.1 = (bf16[128,1536]{1,0:T(8,128)(2,1)S(1)}, bf16[128,1536]{1,0:T(8,128)(2,1)}, u32[]{:S(2)}) copy-start(bf16[128,1536]{1,0:T(8,128)(2,1)} %param.13) | copy-start | bytes 1179652
  212.3 70.7 %copy-start.2 = (f32[1536]{0:T(1024)S(1)}, f32[1536]{0:T(1024)}, u32[]{:S(2)}) copy-start(f32[1536]{0:T(1024)} %param.23) | copy-start | bytes 18436
  212.3 72.0 %all-gather.9.cloned.1.call-start = ((), (), s32[]{:S(2)}) async-start(), calls=%async_computation.5 | async-start | bytes 2433024 | tf_op jit(solution)/shard_map/all_gather | solution.py:75
  212.9 96.7 %all-gather.11.cloned.1.call-start = ((), (), s32[]{:S(2)}) async-start(), calls=%async_computation.6 | async-start | bytes 2433024 | tf_op jit(solution)/shard_map/all_gather | solution.py:78
  213.5 141.4 %all-gather.7.cloned.1.call-start = ((), (), s32[]{:S(2)}) async-start(), calls=%async_computation.4 | async-start | bytes 3538944 | tf_op jit(solution)/shard_map/all_gather | solution.py:74
  284.0 157.1 %reduce-scatter.5.cloned.1.call-start = ((), (), s32[]{:S(2)}) async-start(), calls=%async_computation.7 | async-start | bytes 7077888 | tf_op jit(solution)/shard_map/reduce_scatter | solution.py:80
Sparse Core Ops, SparseCore 0:
  12.0 48.5 all-gather.4
  212.5 68.8 reduce-scatter.2
Sparse Core Ops, SparseCore 1:
  215.4 43.3 all-gather.8
  261.1 48.4 all-gather.10
  311.3 43.5 all-gather.6
  367.1 74.1 reduce-scatter.4
where the time goes:
time: 451 us
  waiting for transfers between devices  262 us (58%)
  blocking collectives  127 us (28%)
  matrix products  20.5 us (5%)
  other arithmetic  17.6 us (4%)
  between operations  15.9 us (4%)
  starting transfers between devices  6.2 us (1%)
    reduce_scatter x1, waiting for transfers between devices, shards(): lax.psum_scatter(partial_out, 'tensor', scatter_dimension=0, tiled=True)  74.2 us
    reduce_scatter x1, waiting for transfers between devices, shards(): lax.psum_scatter(jnp.dot(swished, out_weight, preferred_element_type=jnp....  67.8 us
    psum x1, blocking collectives, shards(): lax.psum(jnp.sum(jnp.square(centred) * valid[:, None], axis=0), 'tm')  65.3 us
    psum x1, blocking collectives, shards(): total, count = lax.psum((first_sum, count_local), 'tm')  61.4 us
    all_gather x1, waiting for transfers between devices, shards(): piece = lax.all_gather(normed, 'tensor', axis=0, tiled=True)  45.6 us
    all_gather x1, waiting for transfers between devices, shards(): feed_block = lax.all_gather(feed_normed, 'tensor', axis=0, tiled=True)  45.3 us
    all_gather x1, waiting for transfers between devices, shards(): down_whole = lax.all_gather(down_weight, 'tm', axis=1, tiled=True)  25.3 us
    dot_general x1, matrix products, shards(): jnp.dot(hidden, down_whole, preferred_element_type=jnp.float32)  12.1 us
  transfers between devices with their start and end apart: 8, of which 6 were waited for; matrix products, arithmetic and copies ran while one was open for 1% of the time, Pallas kernels for 0%

commit v1 on v0

--- a/solution.py
+++ b/solution.py
@@ -46,7 +46,9 @@
     positions = lax.axis_index("tm") * block + jnp.arange(block, dtype=jnp.int32)
     valid = ((frame_mask > 0) & (positions < total_length[0])).astype(jnp.float32)
     normed = layer_norm(features, norm_gain).astype(jnp.bfloat16)
-    piece = lax.all_gather(normed, "tensor", axis=0, tiled=True)
+    piece = jnp.concatenate(
+        lax.all_to_all(jnp.stack([normed] * lax.axis_size("tensor")), "tensor", 0, 0), axis=0
+    )
     value = jnp.dot(piece, value_weight, preferred_element_type=jnp.float32)
     gate = jnp.dot(piece, gate_weight, preferred_element_type=jnp.float32)
     glu = (value * jax.nn.sigmoid(gate) * valid[:, None]).astype(jnp.bfloat16)

time: 451 us -> 486 us (1.078)
  waiting for transfers between devices: 262 us -> 288 us
  starting transfers between devices: 6.2 us -> 14.9 us
    all_to_all x0 -> x1, waiting for transfers between devices: none -> 73 us  [shards(): lax.all_to_all(jnp.stack([normed] * lax.axis_size('tensor')), 'tensor', 0...]
    all_gather x1 -> x0, waiting for transfers between devices: 45.6 us -> none  [shards(): piece = lax.all_gather(normed, 'tensor', axis=0, tiled=True)]
    all_to_all x0 -> x1, starting transfers between devices: none -> 9.15 us  [shards(): lax.all_to_all(jnp.stack([normed] * lax.axis_size('tensor')), 'tensor', 0...]
where the time goes in v1:
time: 486 us
  waiting for transfers between devices  288 us (59%)
  blocking collectives  127 us (26%)
  matrix products  22.2 us (5%)
  other arithmetic  16.1 us (3%)
  between operations  15.8 us (3%)
  starting transfers between devices  14.9 us (3%)
    reduce_scatter x1, waiting for transfers between devices, shards(): lax.psum_scatter(partial_out, 'tensor', scatter_dimension=0, tiled=True)  74.4 us
    all_to_all x1, waiting for transfers between devices, shards(): lax.all_to_all(jnp.stack([normed] * lax.axis_size('tensor')), 'tensor', 0...  73 us
    reduce_scatter x1, waiting for transfers between devices, shards(): lax.psum_scatter(jnp.dot(swished, out_weight, preferred_element_type=jnp....  65.2 us
    psum x1, blocking collectives, shards(): lax.psum(jnp.sum(jnp.square(centred) * valid[:, None], axis=0), 'tm')  65.1 us
    psum x1, blocking collectives, shards(): total, count = lax.psum((first_sum, count_local), 'tm')  61.7 us
    all_gather x1, waiting for transfers between devices, shards(): feed_block = lax.all_gather(feed_normed, 'tensor', axis=0, tiled=True)  45.3 us
    all_gather x1, waiting for transfers between devices, shards(): down_whole = lax.all_gather(down_weight, 'tm', axis=1, tiled=True)  25.3 us
    dot_general x1, matrix products, shards(): jnp.dot(hidden, down_whole, preferred_element_type=jnp.float32)  12 us
  transfers between devices with their start and end apart: 8, of which 6 were waited for; matrix products, arithmetic and copies ran while one was open for 1% of the time, Pallas kernels for 0%

profile of v1, /device:TPU:1, one launch (start us, length us, event | category | flops | bytes accessed | tf_op | source)
XLA Modules:
  0.0 485.7 jit_solution(6314348804245181190)
XLA Ops:
  7.4 1.2 convert_reduce_fusion.1
  8.6 1.2 fusion.14
  9.8 1.3 fusion.16
  11.1 1.9 stack.2
  13.1 9.1 %all-to-all-start = ((bf16[8,128,1536]{2,1,0:T(8,128)(2,1)}), bf16[8,128,1536]{2,1,0:T(8,128)(2,1)}, u32[]{:S(2)}, u32[]{:S(2)}) async-start(bf16[8,128,1536]{2,1,0:T(8,128)(2,1)} %stack.2), calls=%async_computation | async-start | bytes 6291456 | tf_op jit(solution)/shard_map/all_to_all | solution.py:50
  23.6 73.0 %all-to-all-done = bf16[8,128,1536]{2,1,0:T(8,128)(2,1)} async-done(((bf16[8,128,1536]{2,1,0:T(8,128)(2,1)}), bf16[8,128,1536]{2,1,0:T(8,128)(2,1)}, u32[]{:S(2)}, u32[]{:S(2)}) %all-to-all-start) | async-done | bytes 3145760 | tf_op jit(solution)/shard_map/all_to_all | solution.py:50
  96.6 3.2 fusion.5
  99.8 3.1 fusion.6
  103.0 3.5 collective-permute-start
  106.5 1.9 collective-permute-start.1
  108.4 3.4 collective-permute-done.1
  111.9 5.6 %multiply_reduce_fusion.1 = (f32[192]{0:T(256)S(1)}, f32[1024,192]{0,1:T(8,128)S(1)}) fusion(f32[1024]{0:T(1024)S(1)} %get-tuple-element.10, f32[192]{0:T(256)S(1)} %bitcast.71, bf16[15,192]{0,1:T(8,128)(2,1)S(1)} %collective-permute-done.1, bf16[1024,192]{0,1:T(8,128)(2,1)S(1)} %fusion.6, f32[192]{0:T(256)S(1)} %bitcast.72, f32[192]{0:T(256)S(1)} %bitcast.43, ...), kind=kLoop, calls=%fused_computation.58 | loop fusion | flops 36175680 | bytes 1219840 | tf_op jit(solution)/shard_map/reduce_sum | solution.py:60
  117.5 61.7 %all-reduce = (f32[192]{0:T(256)S(1)}, f32[]{:T(128)}) all-reduce(f32[192]{0:T(256)S(1)} %get-tuple-element.11, f32[]{:T(128)} %get-tuple-element.9), channel_id=1, replica_groups=mesh['tm'=32,'tensor'=8] {'tm'}, use_global_device_ids=true, to_apply=%region_3.0 | all-reduce | flops 193 | bytes 1544 | tf_op jit(solution)/shard_map/psum | solution.py:61
  180.1 65.1 %psum.23 = f32[192]{0:T(256)S(1)} all-reduce(f32[192]{0:T(256)S(1)} %multiply_reduce_fusion), channel_id=1, replica_groups=mesh['tm'=32,'tensor'=8] {'tm'}, use_global_device_ids=true, to_apply=%region_7.0 | all-reduce | flops 192 | bytes 1536 | tf_op jit(solution)/shard_map/psum | solution.py:64
  245.2 0.7 add_rsqrt_fusion
  245.9 3.9 fusion.19
  251.0 65.2 %reduce-scatter.3.cloned.1.call-done = f32[128,1536]{1,0:T(8,128)} async-done(((f32[1024,1536]{1,0:T(8,128)}), f32[128,1536]{1,0:T(8,128)}) %reduce-scatter.3.cloned.1.call-update) | async-done | bytes 786448 | tf_op jit(solution)/shard_map/reduce_scatter | solution.py:68
  316.2 1.3 convert_reduce_fusion
  317.8 1.0 fusion.13
  319.1 25.3 %all-gather.8.cloned.1.call-done = bf16[768,1536]{0,1:T(8,128)(2,1)} async-done(((bf16[768,48]{0,1:T(8,128)(2,1)}), bf16[768,1536]{0,1:T(8,128)(2,1)}) %all-gather.8.cloned.1.call-update) | async-done | bytes 2359312 | tf_op jit(solution)/shard_map/all_gather | solution.py:80
  344.4 45.3 %all-gather.4.cloned.1.call-done = bf16[1024,1536]{1,0:T(8,128)(2,1)} async-done(((bf16[128,1536]{1,0:T(8,128)(2,1)}), bf16[1024,1536]{1,0:T(8,128)(2,1)}) %all-gather.4.cloned.1.call-update) | async-done | bytes 3145744 | tf_op jit(solution)/shard_map/all_gather | solution.py:76
  389.7 12.0 %fusion = f32[1024,1536]{1,0:T(8,128)} fusion(bf16[768,1536]{0,1:T(8,128)(2,1)} %all-gather.8.cloned.1.call-done, bf16[1024,1536]{1,0:T(8,128)(2,1)} %all-gather.4.cloned.1.call-done, bf16[1536,768]{1,0:T(8,128)(2,1)} %all-gather.6.cloned.1.call-done), kind=kOutput, calls=%fused_computation.29 | convolution fusion | flops 4835770368 | bytes 14155776 | tf_op jit(solution)/shard_map/dot_general | solution.py:81
  401.8 74.4 %reduce-scatter.5.cloned.1.call-done = f32[128,1536]{1,0:T(8,128)} async-done(((f32[1024,1536]{1,0:T(8,128)}), f32[128,1536]{1,0:T(8,128)}) %reduce-scatter.5.cloned.1.call-update) | async-done | bytes 786448 | tf_op jit(solution)/shard_map/reduce_scatter | solution.py:82
  476.2 2.0 fusion.18
  (41 shorter events, 3.5 us)
Async XLA Ops:
  7.4 238.5 %copy-start = (bf16[192,1536]{1,0:T(8,128)(2,1)S(1)}, bf16[192,1536]{1,0:T(8,128)(2,1)}, u32[]{:S(2)}) copy-start(bf16[192,1536]{1,0:T(8,128)(2,1)} %param.22) | copy-start | bytes 1769476
  13.1 9.9 %copy-start.4 = (s32[1024]{0:T(1024)S(1)}, s32[1024]{0:T(1024)}, u32[]{:S(2)}) copy-start(s32[1024]{0:T(1024)} %param.14) | copy-start | bytes 12292
  13.1 10.5 %copy-start.2 = (f32[31,192]{1,0:T(8,128)S(1)}, f32[31,192]{1,0:T(8,128)}, u32[]{:S(2)}) copy-start(f32[31,192]{1,0:T(8,128)} %param.19) | copy-start | bytes 71428
  13.1 83.5 %copy-start.7 = (bf16[1536,192]{0,1:T(8,128)(2,1)S(1)}, bf16[1536,192]{0,1:T(8,128)(2,1)}, u32[]{:S(2)}) copy-start(bf16[1536,192]{0,1:T(8,128)(2,1)} %param.18) | copy-start | bytes 1769476
  13.1 83.5 %all-to-all-start = ((bf16[8,128,1536]{2,1,0:T(8,128)(2,1)}), bf16[8,128,1536]{2,1,0:T(8,128)(2,1)}, u32[]{:S(2)}, u32[]{:S(2)}) async-start(bf16[8,128,1536]{2,1,0:T(8,128)(2,1)} %stack.2), calls=%async_computation | async-start | bytes 6291456 | tf_op jit(solution)/shard_map/all_to_all | solution.py:50
  22.2 294.0 %reduce-scatter.3.cloned.1.call-start = ((), (), s32[]{:S(2)}) async-start(), calls=%async_computation.3 | async-start | bytes 7077888 | tf_op jit(solution)/shard_map/reduce_scatter | solution.py:68
  96.6 3.2 copy-start.8
  99.8 146.1 %copy-start.5 = (f32[192]{0:T(256)S(1)}, f32[192]{0:T(256)}, u32[]{:S(2)}) copy-start(f32[192]{0:T(256)} %param.21) | copy-start | bytes 2308
  99.8 146.1 %copy-start.6 = (f32[192]{0:T(256)S(1)}, f32[192]{0:T(256)}, u32[]{:S(2)}) copy-start(f32[192]{0:T(256)} %param.20) | copy-start | bytes 2308
  103.0 5.5 %collective-permute-start = (bf16[15,192]{0,1:T(8,128)(2,1)S(1)}, bf16[15,192]{0,1:T(8,128)(2,1)S(1)}, u32[]{:S(2)}, u32[]{:S(2)}) collective-permute-start(bf16[15,192]{0,1:T(8,128)(2,1)S(1)} %get-tuple-element.13), channel_id=1, source_target_pairs={{0,8},{8,16},{16,24},{24,32},{32,40},{40,48},{48,56},{56,64},{64,7... | collective-permute-start | bytes 17288 | tf_op jit(solution)/shard_map/ppermute | solution.py:16
  106.5 5.4 %collective-permute-start.1 = (bf16[15,192]{0,1:T(8,128)(2,1)S(1)}, bf16[15,192]{0,1:T(8,128)(2,1)S(1)}, u32[]{:S(2)}, u32[]{:S(2)}) collective-permute-start(bf16[15,192]{0,1:T(8,128)(2,1)S(1)} %get-tuple-element.14), channel_id=1, source_target_pairs={{8,0},{16,8},{24,16},{32,24},{40,32},{48,40},{56,48},{64,56},{72,6... | collective-permute-start | bytes 17288 | tf_op jit(solution)/shard_map/ppermute | solution.py:17
  249.7 66.5 %copy-start.1 = (bf16[128,1536]{1,0:T(8,128)(2,1)S(1)}, bf16[128,1536]{1,0:T(8,128)(2,1)}, u32[]{:S(2)}) copy-start(bf16[128,1536]{1,0:T(8,128)(2,1)} %param.13) | copy-start | bytes 1179652
  249.7 68.1 %copy-start.3 = (f32[1536]{0:T(1024)S(1)}, f32[1536]{0:T(1024)}, u32[]{:S(2)}) copy-start(f32[1536]{0:T(1024)} %param.23) | copy-start | bytes 18436
  249.8 69.3 %all-gather.6.cloned.1.call-start = ((), (), s32[]{:S(2)}) async-start(), calls=%async_computation.5 | async-start | bytes 2433024 | tf_op jit(solution)/shard_map/all_gather | solution.py:77
  250.3 94.1 %all-gather.8.cloned.1.call-start = ((), (), s32[]{:S(2)}) async-start(), calls=%async_computation.6 | async-start | bytes 2433024 | tf_op jit(solution)/shard_map/all_gather | solution.py:80
  250.9 138.8 %all-gather.4.cloned.1.call-start = ((), (), s32[]{:S(2)}) async-start(), calls=%async_computation.4 | async-start | bytes 3538944 | tf_op jit(solution)/shard_map/all_gather | solution.py:76
  318.9 157.3 %reduce-scatter.5.cloned.1.call-start = ((), (), s32[]{:S(2)}) async-start(), calls=%async_computation.7 | async-start | bytes 7077888 | tf_op jit(solution)/shard_map/reduce_scatter | solution.py:82
Sparse Core Ops, SparseCore 0:
  249.9 66.2 reduce-scatter.2
  401.9 74.2 reduce-scatter.4
Sparse Core Ops, SparseCore 1:
  252.8 40.7 all-gather.5
  295.9 48.4 all-gather.7
  346.1 43.5 all-gather.3
